TPU v7x, 512 devices: a whole 4x8x8 slice. The times are simulated.
512 devices in a mesh: gx: 16 (over y, core), gy: 32 (over x, z).
Axes of the slice: x: 4, y: 8, z: 8, core: 2. Of those that a mesh axis runs over, the one named last changes fastest.
Arguments:
- right_side: float32 [128, 262144], P('gx', 'gy'), may hold values from -6 to 6
- initial_guess: float32 [128, 262144], P('gx', 'gy'), may hold values from -1.2 to 1.2
- coefficients: float32 [5, 128, 16384], P(None, 'gx', 'gy'), may hold values from -1 to 2, as said below
Outputs:
- solution: float32 [128, 262144], P('gx', 'gy')
- residual: float32 [128, 262144], P('gx', 'gy')
Inputs may be any that keep to these rules, and one draw needn't show every extreme that they name: `coefficients`: component 0 is the diffusivity, within 0.5 to 2; components 1 to 3 the drift velocities along the three dimensions, within -1 to 1; component 4 the reaction rate, within 0.5 to 2.
All inputs are finite; a program needn't handle non-finite values.
Results may differ from a plain program's by a relative error of at most 0.0003.
Values sent between devices are 32-bit elements; how exact they have to be, the bound alone decides.
No kernel may reach another device: no remote copies, remote signals or barrier semaphores. Data moves between devices by JAX's collectives and lax.ppermute only.
A program may use at most 64 MiB of HBM per device.

v0:
```python
import jax
import jax.numpy as jnp
from jax import lax
from jax.sharding import PartitionSpec as P

NZ = 32
RHS = 16
STEPS = 3
SHIFT = 7.5
SCALE = 4.0


def extended(block, sides, width):
    for axis, dim in sides:
        count = lax.axis_size(axis)
        forward = [(i, i + 1) for i in range(count - 1)]
        backward = [(target, source) for source, target in forward]
        low = lax.ppermute(
            lax.slice_in_dim(block, block.shape[dim] - width, None, axis=dim), axis, forward
        )
        high = lax.ppermute(lax.slice_in_dim(block, 0, width, axis=dim), axis, backward)
        block = jnp.concatenate([low, block, high], axis=dim)
    return block


def operate(padded, coefs):
    diffusivity, drift_x, drift_y, drift_z, reaction = coefs
    center = padded[1:-1, 1:-1]
    x_plus = padded[2:, 1:-1]
    x_minus = padded[:-2, 1:-1]
    y_plus = padded[1:-1, 2:]
    y_minus = padded[1:-1, :-2]
    zero_rim = jnp.zeros(center.shape[:2] + (RHS,), center.dtype)
    z_plus = jnp.concatenate([center[:, :, RHS:], zero_rim], axis=2)
    z_minus = jnp.concatenate([zero_rim, center[:, :, :-RHS]], axis=2)
    beside = x_plus + x_minus + y_plus + y_minus + z_plus + z_minus
    drift = (
        drift_x * (x_plus - x_minus) + drift_y * (y_plus - y_minus) + drift_z * (z_plus - z_minus)
    )
    return (reaction + 6.0 * diffusivity) * center - diffusivity * beside + 0.5 * drift


def widen(table):
    return [jnp.repeat(table[:, :, i * NZ : (i + 1) * NZ], RHS, axis=2) for i in range(5)]


def combine_rhs(field, weights):
    lanes = jnp.kron(jnp.eye(128 // RHS, dtype=jnp.float32), weights)
    flat = field.reshape(-1, 128)
    return jnp.dot(flat, lanes, precision=lax.Precision.HIGHEST).reshape(field.shape)


def per_device(right_side, initial_guess, coefficients):
    rows_x = right_side.shape[0]
    rows_y = right_side.shape[1] // (NZ * RHS)
    width = NZ * RHS
    rhs_field = right_side.reshape(rows_x, rows_y, width)
    guess = initial_guess.reshape(rows_x, rows_y, width)
    coef_local = jnp.transpose(coefficients.reshape(5, rows_x, rows_y, NZ), (1, 2, 0, 3)).reshape(
        rows_x, rows_y, 5 * NZ
    )
    inner_coefs = widen(coef_local)
    guess_pad = extended(guess, (("gx", 0), ("gy", 1)), 1)
    initial_res = rhs_field - operate(guess_pad, inner_coefs)
    krylov = [initial_res]
    current = initial_res
    for step in range(STEPS):
        padded = extended(current, (("gx", 0), ("gy", 1)), 1)
        current = (operate(padded, inner_coefs) - SHIFT * current) / SCALE
        krylov.append(current)
    blocks = len(krylov)
    groups = 128 // RHS
    stacked = jnp.concatenate([v.reshape(-1, 128) for v in krylov], axis=1)
    products = jnp.dot(stacked.T, stacked, precision=lax.Precision.HIGHEST)
    products = products.reshape(blocks, groups, RHS, blocks, groups, RHS)
    diagonal = jnp.eye(groups, dtype=jnp.float32)[None, :, None, None, :, None]
    local_gram = jnp.sum(products * diagonal, axis=(1, 4)).reshape(blocks * RHS, blocks * RHS)
    gram = lax.psum(local_gram, ("gx", "gy"))
    shift_map = SHIFT * jnp.eye(blocks * RHS, STEPS * RHS, dtype=jnp.float32) + SCALE * jnp.eye(
        blocks * RHS, STEPS * RHS, k=-RHS, dtype=jnp.float32
    )
    normal = jnp.dot(
        shift_map.T,
        jnp.dot(gram, shift_map, precision=lax.Precision.HIGHEST),
        precision=lax.Precision.HIGHEST,
    )
    target = jnp.dot(shift_map.T, gram[:, :RHS], precision=lax.Precision.HIGHEST)
    factor = jnp.linalg.cholesky(normal)
    weights = jax.scipy.linalg.cho_solve((factor, True), target)
    solution = guess
    for step in range(STEPS):
        solution = solution + combine_rhs(krylov[step], weights[step * RHS : (step + 1) * RHS])
    update_pad = extended(solution, (("gx", 0), ("gy", 1)), 1)
    residual = rhs_field - operate(update_pad, inner_coefs)
    return (
        solution.reshape(rows_x, rows_y * NZ * RHS),
        residual.reshape(rows_x, rows_y * NZ * RHS),
    )


def solution(mesh):
    placed = (P("gx", "gy"), P("gx", "gy"), P(None, "gx", "gy"))
    return jax.shard_map(
        per_device,
        mesh=mesh,
        in_specs=placed,
        out_specs=(P("gx", "gy"), P("gx", "gy")),
        check_vma=False,
    )
```

profile of v0, /device:TPU:34, one launch (start us, length us, event | category | flops | bytes accessed | tf_op | source)
XLA Modules:
  0.0 240.8 jit_solution(5623281883208357478)
XLA Ops:
  3.9 4.9 %collective-permute-start = (f32[1,16,512]{2,1,0:T(8,128)S(1)}, f32[1,16,512]{2,1,0:T(8,128)S(1)}, u32[]{:S(2)}, u32[]{:S(2)}) collective-permute-start(f32[1,16,512]{2,1,0:T(8,128)S(1)} %slice.224), channel_id=1, source_target_pairs={{32,0},{64,32},{96,64},{128,96},{160,128},{192,160},{224,192},{256... | collective-permute-start | bytes 98312 | tf_op jit(solution)/shard_map/ppermute | solution.py:21
  12.3 10.9 %collective-permute-start.2 = (f32[10,1,512]{2,1,0:T(1,128)S(1)}, f32[10,1,512]{2,1,0:T(1,128)S(1)}, u32[]{:S(2)}, u32[]{:S(2)}) collective-permute-start(f32[10,1,512]{2,1,0:T(1,128)S(1)} %get-tuple-element.16), channel_id=1, source_target_pairs={{1,0},{2,1},{3,2},{4,3},{5,4},{6,5},{7,6},{8,7},{9,8},{10,9},{11,1... | collective-permute-start | bytes 61448 | tf_op jit(solution)/shard_map/ppermute | solution.py:21
  38.2 2.6 %collective-permute-start.4 = (f32[1,16,512]{2,1,0:T(8,128)S(1)}, f32[1,16,512]{2,1,0:T(8,128)S(1)}, u32[]{:S(2)}, u32[]{:S(2)}) collective-permute-start(f32[1,16,512]{2,1,0:T(8,128)S(1)} %get-tuple-element.31), channel_id=1, source_target_pairs={{32,0},{64,32},{96,64},{128,96},{160,128},{192,160},{224,192},{256... | collective-permute-start | bytes 98312 | tf_op jit(solution)/shard_map/ppermute | solution.py:21
  42.8 4.5 %collective-permute-done.5 = f32[1,16,512]{2,1,0:T(8,128)S(1)} collective-permute-done((f32[1,16,512]{2,1,0:T(8,128)S(1)}, f32[1,16,512]{2,1,0:T(8,128)S(1)}, u32[]{:S(2)}, u32[]{:S(2)}) %collective-permute-start.5) | collective-permute-done | bytes 32800 | tf_op jit(solution)/shard_map/ppermute | solution.py:18
  47.3 5.8 %collective-permute-start.6 = (f32[10,1,512]{2,1,0:T(1,128)S(1)}, f32[10,1,512]{2,1,0:T(1,128)S(1)}, u32[]{:S(2)}, u32[]{:S(2)}) collective-permute-start(f32[10,1,512]{2,1,0:T(1,128)S(1)} %get-tuple-element.14), channel_id=1, source_target_pairs={{1,0},{2,1},{3,2},{4,3},{5,4},{6,5},{7,6},{8,7},{9,8},{10,9},{11,1... | collective-permute-start | bytes 61448 | tf_op jit(solution)/shard_map/ppermute | solution.py:21
  55.3 5.5 %collective-permute-done.7 = f32[10,1,512]{2,1,0:T(1,128)S(1)} collective-permute-done((f32[10,1,512]{2,1,0:T(1,128)S(1)}, f32[10,1,512]{2,1,0:T(1,128)S(1)}, u32[]{:S(2)}, u32[]{:S(2)}) %collective-permute-start.7) | collective-permute-done | bytes 20512 | tf_op jit(solution)/shard_map/ppermute | solution.py:18
  63.1 2.4 collective-permute-start.9
  65.5 4.0 %collective-permute-done.9 = f32[1,16,512]{2,1,0:T(8,128)S(1)} collective-permute-done((f32[1,16,512]{2,1,0:T(8,128)S(1)}, f32[1,16,512]{2,1,0:T(8,128)S(1)}, u32[]{:S(2)}, u32[]{:S(2)}) %collective-permute-start.9) | collective-permute-done | bytes 32800 | tf_op jit(solution)/shard_map/ppermute | solution.py:18
  71.5 3.9 %collective-permute-start.11 = (f32[10,1,512]{2,1,0:T(1,128)S(1)}, f32[10,1,512]{2,1,0:T(1,128)S(1)}, u32[]{:S(2)}, u32[]{:S(2)}) collective-permute-start(f32[10,1,512]{2,1,0:T(1,128)S(1)} %get-tuple-element.13), channel_id=1, source_target_pairs={{0,1},{1,2},{2,3},{3,4},{4,5},{5,6},{6,7},{7,8},{8,9},{9,10},{10,1... | collective-permute-start | bytes 61448 | tf_op jit(solution)/shard_map/ppermute | solution.py:18
  75.6 3.7 %collective-permute-done.11 = f32[10,1,512]{2,1,0:T(1,128)S(1)} collective-permute-done((f32[10,1,512]{2,1,0:T(1,128)S(1)}, f32[10,1,512]{2,1,0:T(1,128)S(1)}, u32[]{:S(2)}, u32[]{:S(2)}) %collective-permute-start.11) | collective-permute-done | bytes 20512 | tf_op jit(solution)/shard_map/ppermute | solution.py:18
  81.6 2.4 collective-permute-start.13
  84.1 4.0 %collective-permute-done.13 = f32[1,16,512]{2,1,0:T(8,128)S(1)} collective-permute-done((f32[1,16,512]{2,1,0:T(8,128)S(1)}, f32[1,16,512]{2,1,0:T(8,128)S(1)}, u32[]{:S(2)}, u32[]{:S(2)}) %collective-permute-start.13) | collective-permute-done | bytes 32800 | tf_op jit(solution)/shard_map/ppermute | solution.py:18
  90.0 3.9 %collective-permute-start.15 = (f32[10,1,512]{2,1,0:T(1,128)S(1)}, f32[10,1,512]{2,1,0:T(1,128)S(1)}, u32[]{:S(2)}, u32[]{:S(2)}) collective-permute-start(f32[10,1,512]{2,1,0:T(1,128)S(1)} %get-tuple-element.11), channel_id=1, source_target_pairs={{0,1},{1,2},{2,3},{3,4},{4,5},{5,6},{6,7},{7,8},{8,9},{9,10},{10,1... | collective-permute-start | bytes 61448 | tf_op jit(solution)/shard_map/ppermute | solution.py:18
  94.1 3.7 %collective-permute-done.15 = f32[10,1,512]{2,1,0:T(1,128)S(1)} collective-permute-done((f32[10,1,512]{2,1,0:T(1,128)S(1)}, f32[10,1,512]{2,1,0:T(1,128)S(1)}, u32[]{:S(2)}, u32[]{:S(2)}) %collective-permute-start.15) | collective-permute-done | bytes 20512 | tf_op jit(solution)/shard_map/ppermute | solution.py:18
  100.0 4.9 %reshape.161 = f32[4,8,16,4,8,16]{5,4,3,2,1,0:T(8,128)} reshape(f32[512,512]{1,0:T(8,128)S(1)} %fusion) | data formatting | bytes 2097152 | tf_op jit(solution)/shard_map/reshape | solution.py:75
  104.9 4.8 %multiply_reduce_fusion = f32[4,16,4,16]{3,2,1,0:T(4,128)S(1)} fusion(f32[4,8,16,4,8,16]{5,4,3,2,1,0:T(8,128)} %reshape.161, f32[8,8]{1,0:T(8,128)S(1)} %fusion.31), kind=kLoop, calls=%fused_computation | loop fusion | flops 520192 | bytes 1065216 | tf_op jit(solution)/shard_map/reduce_sum | solution.py:77
  109.8 93.3 %psum.7 = f32[64,64]{1,0:T(8,128)S(1)} all-reduce(f32[64,64]{1,0:T(8,128)S(1)} %reshape.162), channel_id=1, replica_groups=mesh['gx'=16,'gy'=32] {'gx','gy'}, use_global_device_ids=true, to_apply=%region_1.0 | all-reduce | flops 4096 | bytes 32768 | tf_op jit(solution)/shard_map/psum | solution.py:78
  204.0 4.4 %cholesky.16 = f32[48,48]{1,0:T(8,128)S(1)} custom-call(f32[48,48]{1,0:T(8,128)S(1)} %fusion.18), custom_call_target="Cholesky" | custom-call | tf_op jit(solution)/shard_map/jit(cholesky)/cholesky | solution.py:88
  209.8 3.7 %custom-call.10 = f32[1,48,48]{1,2,0:T(8,128)S(1)} custom-call(f32[1,48,48]{2,1,0:T(8,128)S(1)} %fusion.13), custom_call_target="InvertDiagBlocksLowerTriangular" | custom-call | tf_op jit(solution)/shard_map/jit(_cho_solve)/triangular_solve | solution.py:89
  217.7 4.1 %collective-permute-start.16 = (f32[1,16,512]{2,1,0:T(8,128)S(1)}, f32[1,16,512]{2,1,0:T(8,128)S(1)}, u32[]{:S(2)}, u32[]{:S(2)}) collective-permute-start(f32[1,16,512]{2,1,0:T(8,128)S(1)} %get-tuple-element.19), channel_id=1, source_target_pairs={{32,0},{64,32},{96,64},{128,96},{160,128},{192,160},{224,192},{256... | collective-permute-start | bytes 98312 | tf_op jit(solution)/shard_map/ppermute | solution.py:21
  224.5 3.8 %collective-permute-done.17 = f32[1,16,512]{2,1,0:T(8,128)S(1)} collective-permute-done((f32[1,16,512]{2,1,0:T(8,128)S(1)}, f32[1,16,512]{2,1,0:T(8,128)S(1)}, u32[]{:S(2)}, u32[]{:S(2)}) %collective-permute-start.17) | collective-permute-done | bytes 32800 | tf_op jit(solution)/shard_map/ppermute | solution.py:18
  228.3 3.4 %collective-permute-start.18 = (f32[10,1,512]{2,1,0:T(1,128)S(1)}, f32[10,1,512]{2,1,0:T(1,128)S(1)}, u32[]{:S(2)}, u32[]{:S(2)}) collective-permute-start(f32[10,1,512]{2,1,0:T(1,128)S(1)} %get-tuple-element.8), channel_id=1, source_target_pairs={{1,0},{2,1},{3,2},{4,3},{5,4},{6,5},{7,6},{8,7},{9,8},{10,9},{11,1... | collective-permute-start | bytes 61448 | tf_op jit(solution)/shard_map/ppermute | solution.py:21
  231.7 2.4 %collective-permute-start.19 = (f32[10,1,512]{2,1,0:T(1,128)S(1)}, f32[10,1,512]{2,1,0:T(1,128)S(1)}, u32[]{:S(2)}, u32[]{:S(2)}) collective-permute-start(f32[10,1,512]{2,1,0:T(1,128)S(1)} %get-tuple-element.9), channel_id=1, source_target_pairs={{0,1},{1,2},{2,3},{3,4},{4,5},{5,6},{6,7},{7,8},{8,9},{9,10},{10,1... | collective-permute-start | bytes 61448 | tf_op jit(solution)/shard_map/ppermute | solution.py:18
  234.3 5.2 %collective-permute-done.19 = f32[10,1,512]{2,1,0:T(1,128)S(1)} collective-permute-done((f32[10,1,512]{2,1,0:T(1,128)S(1)}, f32[10,1,512]{2,1,0:T(1,128)S(1)}, u32[]{:S(2)}, u32[]{:S(2)}) %collective-permute-start.19) | collective-permute-done | bytes 20512 | tf_op jit(solution)/shard_map/ppermute | solution.py:18
  (111 shorter events, 47.4 us)
Async XLA Ops:
  0.6 11.5 %copy-start = (f32[8,8192]{1,0:T(8,128)S(1)}, f32[8,8192]{1,0:T(8,128)}, u32[]{:S(2)}) copy-start(f32[8,8192]{1,0:T(8,128)} %param.4) | copy-start | bytes 786436
  1.9 10.2 %collective-permute-start.1 = (f32[1,16,512]{2,1,0:T(8,128)S(1)}, f32[1,16,512]{2,1,0:T(8,128)S(1)}, u32[]{:S(2)}, u32[]{:S(2)}) collective-permute-start(f32[1,16,512]{2,1,0:T(8,128)S(1)} %slice.227), channel_id=1, source_target_pairs={{0,32},{32,64},{64,96},{96,128},{128,160},{160,192},{192,224},{224... | collective-permute-start | bytes 98312 | tf_op jit(solution)/shard_map/ppermute | solution.py:18
  3.9 8.4 %collective-permute-start = (f32[1,16,512]{2,1,0:T(8,128)S(1)}, f32[1,16,512]{2,1,0:T(8,128)S(1)}, u32[]{:S(2)}, u32[]{:S(2)}) collective-permute-start(f32[1,16,512]{2,1,0:T(8,128)S(1)} %slice.224), channel_id=1, source_target_pairs={{32,0},{64,32},{96,64},{128,96},{160,128},{192,160},{224,192},{256... | collective-permute-start | bytes 98312 | tf_op jit(solution)/shard_map/ppermute | solution.py:21
  9.8 15.5 %copy-start.2 = (f32[1,8,16,512]{3,2,1,0:T(8,128)}, f32[1,8,16,512]{3,2,1,0:T(8,128)S(1)}, u32[]{:S(2)}) copy-start(f32[1,8,16,512]{3,2,1,0:T(8,128)S(1)} %copy.35) | copy-start | bytes 786436
  12.3 15.2 %copy-start.5 = (f32[10,16,512]{2,1,0:T(8,128)}, f32[10,16,512]{2,1,0:T(8,128)S(1)}, u32[]{:S(2)}) copy-start(f32[10,16,512]{2,1,0:T(8,128)S(1)} %constant_dynamic-update-slice_fusion) | copy-start | bytes 983044
  12.3 23.8 %collective-permute-start.2 = (f32[10,1,512]{2,1,0:T(1,128)S(1)}, f32[10,1,512]{2,1,0:T(1,128)S(1)}, u32[]{:S(2)}, u32[]{:S(2)}) collective-permute-start(f32[10,1,512]{2,1,0:T(1,128)S(1)} %get-tuple-element.16), channel_id=1, source_target_pairs={{1,0},{2,1},{3,2},{4,3},{5,4},{6,5},{7,6},{8,7},{9,8},{10,9},{11,1... | collective-permute-start | bytes 61448 | tf_op jit(solution)/shard_map/ppermute | solution.py:21
  23.3 12.9 %collective-permute-start.3 = (f32[10,1,512]{2,1,0:T(1,128)S(1)}, f32[10,1,512]{2,1,0:T(1,128)S(1)}, u32[]{:S(2)}, u32[]{:S(2)}) collective-permute-start(f32[10,1,512]{2,1,0:T(1,128)S(1)} %get-tuple-element.17), channel_id=1, source_target_pairs={{0,1},{1,2},{2,3},{3,4},{4,5},{5,6},{6,7},{7,8},{8,9},{9,10},{10,1... | collective-permute-start | bytes 61448 | tf_op jit(solution)/shard_map/ppermute | solution.py:18
  38.2 4.5 %collective-permute-start.4 = (f32[1,16,512]{2,1,0:T(8,128)S(1)}, f32[1,16,512]{2,1,0:T(8,128)S(1)}, u32[]{:S(2)}, u32[]{:S(2)}) collective-permute-start(f32[1,16,512]{2,1,0:T(8,128)S(1)} %get-tuple-element.31), channel_id=1, source_target_pairs={{32,0},{64,32},{96,64},{128,96},{160,128},{192,160},{224,192},{256... | collective-permute-start | bytes 98312 | tf_op jit(solution)/shard_map/ppermute | solution.py:21
  40.8 6.4 %collective-permute-start.5 = (f32[1,16,512]{2,1,0:T(8,128)S(1)}, f32[1,16,512]{2,1,0:T(8,128)S(1)}, u32[]{:S(2)}, u32[]{:S(2)}) collective-permute-start(f32[1,16,512]{2,1,0:T(8,128)S(1)} %get-tuple-element.30), channel_id=1, source_target_pairs={{0,32},{32,64},{64,96},{96,128},{128,160},{160,192},{192,224},{224... | collective-permute-start | bytes 98312 | tf_op jit(solution)/shard_map/ppermute | solution.py:18
  47.3 8.0 %collective-permute-start.6 = (f32[10,1,512]{2,1,0:T(1,128)S(1)}, f32[10,1,512]{2,1,0:T(1,128)S(1)}, u32[]{:S(2)}, u32[]{:S(2)}) collective-permute-start(f32[10,1,512]{2,1,0:T(1,128)S(1)} %get-tuple-element.14), channel_id=1, source_target_pairs={{1,0},{2,1},{3,2},{4,3},{5,4},{6,5},{7,6},{8,7},{9,8},{10,9},{11,1... | collective-permute-start | bytes 61448 | tf_op jit(solution)/shard_map/ppermute | solution.py:21
  53.1 7.8 %collective-permute-start.7 = (f32[10,1,512]{2,1,0:T(1,128)S(1)}, f32[10,1,512]{2,1,0:T(1,128)S(1)}, u32[]{:S(2)}, u32[]{:S(2)}) collective-permute-start(f32[10,1,512]{2,1,0:T(1,128)S(1)} %get-tuple-element.15), channel_id=1, source_target_pairs={{0,1},{1,2},{2,3},{3,4},{4,5},{5,6},{6,7},{7,8},{8,9},{9,10},{10,1... | collective-permute-start | bytes 61448 | tf_op jit(solution)/shard_map/ppermute | solution.py:18
  61.2 4.4 %collective-permute-start.8 = (f32[1,16,512]{2,1,0:T(8,128)S(1)}, f32[1,16,512]{2,1,0:T(8,128)S(1)}, u32[]{:S(2)}, u32[]{:S(2)}) collective-permute-start(f32[1,16,512]{2,1,0:T(8,128)S(1)} %get-tuple-element.27), channel_id=1, source_target_pairs={{32,0},{64,32},{96,64},{128,96},{160,128},{192,160},{224,192},{256... | collective-permute-start | bytes 98312 | tf_op jit(solution)/shard_map/ppermute | solution.py:21
  63.1 6.4 %collective-permute-start.9 = (f32[1,16,512]{2,1,0:T(8,128)S(1)}, f32[1,16,512]{2,1,0:T(8,128)S(1)}, u32[]{:S(2)}, u32[]{:S(2)}) collective-permute-start(f32[1,16,512]{2,1,0:T(8,128)S(1)} %get-tuple-element.26), channel_id=1, source_target_pairs={{0,32},{32,64},{64,96},{96,128},{128,160},{160,192},{192,224},{224... | collective-permute-start | bytes 98312 | tf_op jit(solution)/shard_map/ppermute | solution.py:18
  69.6 6.0 %collective-permute-start.10 = (f32[10,1,512]{2,1,0:T(1,128)S(1)}, f32[10,1,512]{2,1,0:T(1,128)S(1)}, u32[]{:S(2)}, u32[]{:S(2)}) collective-permute-start(f32[10,1,512]{2,1,0:T(1,128)S(1)} %get-tuple-element.12), channel_id=1, source_target_pairs={{1,0},{2,1},{3,2},{4,3},{5,4},{6,5},{7,6},{8,7},{9,8},{10,9},{11,1... | collective-permute-start | bytes 61448 | tf_op jit(solution)/shard_map/ppermute | solution.py:21
  71.5 7.8 %collective-permute-start.11 = (f32[10,1,512]{2,1,0:T(1,128)S(1)}, f32[10,1,512]{2,1,0:T(1,128)S(1)}, u32[]{:S(2)}, u32[]{:S(2)}) collective-permute-start(f32[10,1,512]{2,1,0:T(1,128)S(1)} %get-tuple-element.13), channel_id=1, source_target_pairs={{0,1},{1,2},{2,3},{3,4},{4,5},{5,6},{6,7},{7,8},{8,9},{9,10},{10,1... | collective-permute-start | bytes 61448 | tf_op jit(solution)/shard_map/ppermute | solution.py:18
  79.6 4.4 %collective-permute-start.12 = (f32[1,16,512]{2,1,0:T(8,128)S(1)}, f32[1,16,512]{2,1,0:T(8,128)S(1)}, u32[]{:S(2)}, u32[]{:S(2)}) collective-permute-start(f32[1,16,512]{2,1,0:T(8,128)S(1)} %get-tuple-element.23), channel_id=1, source_target_pairs={{32,0},{64,32},{96,64},{128,96},{160,128},{192,160},{224,192},{256... | collective-permute-start | bytes 98312 | tf_op jit(solution)/shard_map/ppermute | solution.py:21
  81.6 6.4 %collective-permute-start.13 = (f32[1,16,512]{2,1,0:T(8,128)S(1)}, f32[1,16,512]{2,1,0:T(8,128)S(1)}, u32[]{:S(2)}, u32[]{:S(2)}) collective-permute-start(f32[1,16,512]{2,1,0:T(8,128)S(1)} %get-tuple-element.22), channel_id=1, source_target_pairs={{0,32},{32,64},{64,96},{96,128},{128,160},{160,192},{192,224},{224... | collective-permute-start | bytes 98312 | tf_op jit(solution)/shard_map/ppermute | solution.py:18
  88.1 6.0 %collective-permute-start.14 = (f32[10,1,512]{2,1,0:T(1,128)S(1)}, f32[10,1,512]{2,1,0:T(1,128)S(1)}, u32[]{:S(2)}, u32[]{:S(2)}) collective-permute-start(f32[10,1,512]{2,1,0:T(1,128)S(1)} %get-tuple-element.10), channel_id=1, source_target_pairs={{1,0},{2,1},{3,2},{4,3},{5,4},{6,5},{7,6},{8,7},{9,8},{10,9},{11,1... | collective-permute-start | bytes 61448 | tf_op jit(solution)/shard_map/ppermute | solution.py:21
  90.0 7.8 %collective-permute-start.15 = (f32[10,1,512]{2,1,0:T(1,128)S(1)}, f32[10,1,512]{2,1,0:T(1,128)S(1)}, u32[]{:S(2)}, u32[]{:S(2)}) collective-permute-start(f32[10,1,512]{2,1,0:T(1,128)S(1)} %get-tuple-element.11), channel_id=1, source_target_pairs={{0,1},{1,2},{2,3},{3,4},{4,5},{5,6},{6,7},{7,8},{8,9},{9,10},{10,1... | collective-permute-start | bytes 61448 | tf_op jit(solution)/shard_map/ppermute | solution.py:18
  217.4 22.1 %copy-start.4 = (f32[8,8192]{1,0:T(8,128)S(1)}, f32[8,8192]{1,0:T(8,128)}, u32[]{:S(2)}) copy-start(f32[8,8192]{1,0:T(8,128)} %param.3) | copy-start | bytes 786436
  217.7 6.8 %collective-permute-start.16 = (f32[1,16,512]{2,1,0:T(8,128)S(1)}, f32[1,16,512]{2,1,0:T(8,128)S(1)}, u32[]{:S(2)}, u32[]{:S(2)}) collective-permute-start(f32[1,16,512]{2,1,0:T(8,128)S(1)} %get-tuple-element.19), channel_id=1, source_target_pairs={{32,0},{64,32},{96,64},{128,96},{160,128},{192,160},{224,192},{256... | collective-permute-start | bytes 98312 | tf_op jit(solution)/shard_map/ppermute | solution.py:21
  221.8 6.4 %collective-permute-start.17 = (f32[1,16,512]{2,1,0:T(8,128)S(1)}, f32[1,16,512]{2,1,0:T(8,128)S(1)}, u32[]{:S(2)}, u32[]{:S(2)}) collective-permute-start(f32[1,16,512]{2,1,0:T(8,128)S(1)} %get-tuple-element.18), channel_id=1, source_target_pairs={{0,32},{32,64},{64,96},{96,128},{128,160},{160,192},{192,224},{224... | collective-permute-start | bytes 98312 | tf_op jit(solution)/shard_map/ppermute | solution.py:18
  228.3 6.0 %collective-permute-start.18 = (f32[10,1,512]{2,1,0:T(1,128)S(1)}, f32[10,1,512]{2,1,0:T(1,128)S(1)}, u32[]{:S(2)}, u32[]{:S(2)}) collective-permute-start(f32[10,1,512]{2,1,0:T(1,128)S(1)} %get-tuple-element.8), channel_id=1, source_target_pairs={{1,0},{2,1},{3,2},{4,3},{5,4},{6,5},{7,6},{8,7},{9,8},{10,9},{11,1... | collective-permute-start | bytes 61448 | tf_op jit(solution)/shard_map/ppermute | solution.py:21
  231.7 7.8 %collective-permute-start.19 = (f32[10,1,512]{2,1,0:T(1,128)S(1)}, f32[10,1,512]{2,1,0:T(1,128)S(1)}, u32[]{:S(2)}, u32[]{:S(2)}) collective-permute-start(f32[10,1,512]{2,1,0:T(1,128)S(1)} %get-tuple-element.9), channel_id=1, source_target_pairs={{0,1},{1,2},{2,3},{3,4},{4,5},{5,6},{6,7},{7,8},{8,9},{9,10},{10,1... | collective-permute-start | bytes 61448 | tf_op jit(solution)/shard_map/ppermute | solution.py:18
  (2 other events, 8.2 us)
where the time goes:
time: 242 us; the launch traced here: 241 us
  blocking collectives  93.3 us (39%)
  starting transfers between devices  64.2 us (27%)
  waiting for transfers between devices  34.4 us (14%)
  local copies, waits for them, and re-layouts  23.5 us (10%)
  other arithmetic  19 us (8%)
  matrix products  5.16 us (2%)
    psum x1, blocking collectives, per_device(): gram = lax.psum(local_gram, ('gx', 'gy'))  93.3 us
    ppermute x10, starting transfers between devices, extended(): lax.ppermute(lax.slice_in_dim(block, 0, width, axis=dim), axis, backward)  39.3 us
    ppermute x10, waiting for transfers between devices, extended(): lax.ppermute(lax.slice_in_dim(block, block.shape[dim] - width, None, axis...  34.3 us
    ppermute x10, starting transfers between devices, extended(): lax.ppermute(lax.slice_in_dim(block, block.shape[dim] - width, None, axis...  24.9 us
    reshape x5, local copies, waits for them, and re-layouts, widen(): jnp.repeat(table[:, :, i * NZ:(i + 1) * NZ], RHS, axis=2)  7.77 us
    another operation x3, other arithmetic, per_device(): factor = jnp.linalg.cholesky(normal)  5.05 us
    reshape x1, local copies, waits for them, and re-layouts, per_device(): products = products.reshape(blocks, groups, RHS, blocks, groups, RHS)  4.93 us
  transfers between devices with their start and end apart: 20, of which 8 were waited for; matrix products, arithmetic and copies ran while one was open for 7% of the time, Pallas kernels for 0%

commit v1 on v0

--- a/solution.py
+++ b/solution.py
@@ -75,7 +75,7 @@
     products = products.reshape(blocks, groups, RHS, blocks, groups, RHS)
     diagonal = jnp.eye(groups, dtype=jnp.float32)[None, :, None, None, :, None]
     local_gram = jnp.sum(products * diagonal, axis=(1, 4)).reshape(blocks * RHS, blocks * RHS)
-    gram = lax.psum(local_gram, ("gx", "gy"))
+    gram = jnp.sum(lax.all_gather(local_gram, ("gx", "gy")), axis=0)
     shift_map = SHIFT * jnp.eye(blocks * RHS, STEPS * RHS, dtype=jnp.float32) + SCALE * jnp.eye(
         blocks * RHS, STEPS * RHS, k=-RHS, dtype=jnp.float32
     )

time: 242 us -> 305 us (1.26)
  waiting for transfers between devices: 34.4 us -> 163 us
  blocking collectives: 93.3 us -> 0 us
  between operations: 1.34 us -> 14.7 us
  other arithmetic: 19 us -> 28 us
    all_gather x0 -> x1, waiting for transfers between devices: none -> 129 us  [per_device(): gram = jnp.sum(lax.all_gather(local_gram, ('gx', 'gy')), axis=0)]
    psum x1 -> x0, blocking collectives: 93.3 us -> none  [per_device(): gram = lax.psum(local_gram, ('gx', 'gy'))]
    reduce_sum x0 -> x1, other arithmetic: none -> 6.94 us  [per_device(): gram = jnp.sum(lax.all_gather(local_gram, ('gx', 'gy')), axis=0)]
  transfers between devices with their start and end apart: 20 -> 21, of which waited for: 8 -> 9; matrix products, arithmetic and copies ran while one was open for 7% -> 6% of each run, Pallas kernels for 0% -> 0%
where the time goes in v1:
time: 305 us; the launch traced here: 303 us
  waiting for transfers between devices  163 us (53%)
  starting transfers between devices  64.5 us (21%)
  other arithmetic  28 us (9%)
  local copies, waits for them, and re-layouts  26.4 us (9%)
  between operations  14.7 us (5%)
  matrix products  6.93 us (2%)
    all_gather x1, waiting for transfers between devices, per_device(): gram = jnp.sum(lax.all_gather(local_gram, ('gx', 'gy')), axis=0)  129 us
    ppermute x10, starting transfers between devices, extended(): lax.ppermute(lax.slice_in_dim(block, 0, width, axis=dim), axis, backward)  39.7 us
    ppermute x10, waiting for transfers between devices, extended(): lax.ppermute(lax.slice_in_dim(block, block.shape[dim] - width, None, axis...  34.3 us
    ppermute x10, starting transfers between devices, extended(): lax.ppermute(lax.slice_in_dim(block, block.shape[dim] - width, None, axis...  24.8 us
    reshape x5, local copies, waits for them, and re-layouts, widen(): jnp.repeat(table[:, :, i * NZ:(i + 1) * NZ], RHS, axis=2)  7.77 us
    reduce_sum x1, other arithmetic, per_device(): gram = jnp.sum(lax.all_gather(local_gram, ('gx', 'gy')), axis=0)  6.94 us
  transfers between devices with their start and end apart: 21, of which 9 were waited for; matrix products, arithmetic and copies ran while one was open for 6% of the time, Pallas kernels for 0%

profile of v1, /device:TPU:34, one launch (start us, length us, event | category | flops | bytes accessed | tf_op | source)
XLA Modules:
  0.0 303.5 jit_solution(8978388759258726462)
XLA Ops:
  10.4 4.9 %collective-permute-start = (f32[1,16,512]{2,1,0:T(8,128)S(1)}, f32[1,16,512]{2,1,0:T(8,128)S(1)}, u32[]{:S(2)}, u32[]{:S(2)}) collective-permute-start(f32[1,16,512]{2,1,0:T(8,128)S(1)} %slice.224), channel_id=1, source_target_pairs={{32,0},{64,32},{96,64},{128,96},{160,128},{192,160},{224,192},{256... | collective-permute-start | bytes 98312 | tf_op jit(solution)/shard_map/ppermute | solution.py:21
  20.5 10.9 %collective-permute-start.2 = (f32[10,1,512]{2,1,0:T(1,128)}, f32[10,1,512]{2,1,0:T(1,128)}, u32[]{:S(2)}, u32[]{:S(2)}) collective-permute-start(f32[10,1,512]{2,1,0:T(1,128)} %get-tuple-element.16), channel_id=1, source_target_pairs={{1,0},{2,1},{3,2},{4,3},{5,4},{6,5},{7,6},{8,7},{9,8},{10,9},{11,1... | collective-permute-start | bytes 61448 | tf_op jit(solution)/shard_map/ppermute | solution.py:21
  48.3 2.4 collective-permute-start.5
  50.7 4.0 %collective-permute-done.5 = f32[1,16,512]{2,1,0:T(8,128)S(1)} collective-permute-done((f32[1,16,512]{2,1,0:T(8,128)S(1)}, f32[1,16,512]{2,1,0:T(8,128)S(1)}, u32[]{:S(2)}, u32[]{:S(2)}) %collective-permute-start.5) | collective-permute-done | bytes 32800 | tf_op jit(solution)/shard_map/ppermute | solution.py:18
  54.8 6.0 %collective-permute-start.6 = (f32[10,1,512]{2,1,0:T(1,128)S(1)}, f32[10,1,512]{2,1,0:T(1,128)S(1)}, u32[]{:S(2)}, u32[]{:S(2)}) collective-permute-start(f32[10,1,512]{2,1,0:T(1,128)S(1)} %get-tuple-element.14), channel_id=1, source_target_pairs={{1,0},{2,1},{3,2},{4,3},{5,4},{6,5},{7,6},{8,7},{9,8},{10,9},{11,1... | collective-permute-start | bytes 61448 | tf_op jit(solution)/shard_map/ppermute | solution.py:21
  63.1 5.5 %collective-permute-done.7 = f32[10,1,512]{2,1,0:T(1,128)S(1)} collective-permute-done((f32[10,1,512]{2,1,0:T(1,128)S(1)}, f32[10,1,512]{2,1,0:T(1,128)S(1)}, u32[]{:S(2)}, u32[]{:S(2)}) %collective-permute-start.7) | collective-permute-done | bytes 20512 | tf_op jit(solution)/shard_map/ppermute | solution.py:18
  70.9 2.4 collective-permute-start.9
  73.3 4.0 %collective-permute-done.9 = f32[1,16,512]{2,1,0:T(8,128)S(1)} collective-permute-done((f32[1,16,512]{2,1,0:T(8,128)S(1)}, f32[1,16,512]{2,1,0:T(8,128)S(1)}, u32[]{:S(2)}, u32[]{:S(2)}) %collective-permute-start.9) | collective-permute-done | bytes 32800 | tf_op jit(solution)/shard_map/ppermute | solution.py:18
  79.3 3.9 %collective-permute-start.11 = (f32[10,1,512]{2,1,0:T(1,128)S(1)}, f32[10,1,512]{2,1,0:T(1,128)S(1)}, u32[]{:S(2)}, u32[]{:S(2)}) collective-permute-start(f32[10,1,512]{2,1,0:T(1,128)S(1)} %get-tuple-element.13), channel_id=1, source_target_pairs={{0,1},{1,2},{2,3},{3,4},{4,5},{5,6},{6,7},{7,8},{8,9},{9,10},{10,1... | collective-permute-start | bytes 61448 | tf_op jit(solution)/shard_map/ppermute | solution.py:18
  83.4 3.7 %collective-permute-done.11 = f32[10,1,512]{2,1,0:T(1,128)S(1)} collective-permute-done((f32[10,1,512]{2,1,0:T(1,128)S(1)}, f32[10,1,512]{2,1,0:T(1,128)S(1)}, u32[]{:S(2)}, u32[]{:S(2)}) %collective-permute-start.11) | collective-permute-done | bytes 20512 | tf_op jit(solution)/shard_map/ppermute | solution.py:18
  89.3 2.4 collective-permute-start.13
  91.9 3.9 %collective-permute-done.13 = f32[1,16,512]{2,1,0:T(8,128)S(1)} collective-permute-done((f32[1,16,512]{2,1,0:T(8,128)S(1)}, f32[1,16,512]{2,1,0:T(8,128)S(1)}, u32[]{:S(2)}, u32[]{:S(2)}) %collective-permute-start.13) | collective-permute-done | bytes 32800 | tf_op jit(solution)/shard_map/ppermute | solution.py:18
  97.8 3.9 %collective-permute-start.15 = (f32[10,1,512]{2,1,0:T(1,128)S(1)}, f32[10,1,512]{2,1,0:T(1,128)S(1)}, u32[]{:S(2)}, u32[]{:S(2)}) collective-permute-start(f32[10,1,512]{2,1,0:T(1,128)S(1)} %get-tuple-element.11), channel_id=1, source_target_pairs={{0,1},{1,2},{2,3},{3,4},{4,5},{5,6},{6,7},{7,8},{8,9},{9,10},{10,1... | collective-permute-start | bytes 61448 | tf_op jit(solution)/shard_map/ppermute | solution.py:18
  101.9 3.7 %collective-permute-done.15 = f32[10,1,512]{2,1,0:T(1,128)S(1)} collective-permute-done((f32[10,1,512]{2,1,0:T(1,128)S(1)}, f32[10,1,512]{2,1,0:T(1,128)S(1)}, u32[]{:S(2)}, u32[]{:S(2)}) %collective-permute-start.15) | collective-permute-done | bytes 20512 | tf_op jit(solution)/shard_map/ppermute | solution.py:18
  107.8 4.9 %reshape.158 = f32[4,8,16,4,8,16]{5,4,3,2,1,0:T(8,128)} reshape(f32[512,512]{1,0:T(8,128)S(1)} %fusion) | data formatting | bytes 2097152 | tf_op jit(solution)/shard_map/reshape | solution.py:75
  112.7 4.8 %multiply_reduce_fusion = f32[4,16,4,16]{3,2,1,0:T(4,128)S(1)} fusion(f32[4,8,16,4,8,16]{5,4,3,2,1,0:T(8,128)} %reshape.158, f32[8,8]{1,0:T(8,128)S(1)} %fusion.31), kind=kLoop, calls=%fused_computation | loop fusion | flops 520192 | bytes 1065216 | tf_op jit(solution)/shard_map/reduce_sum | solution.py:77
  118.2 128.6 %all-gather.2.cloned.1.call-done = f32[512,64,64]{2,1,0:T(8,128)} async-done(((f32[1,64,64]{2,1,0:T(8,128)}), f32[512,64,64]{2,1,0:T(8,128)}) %all-gather.2.cloned.1.call-update) | async-done | bytes 8388624 | tf_op jit(solution)/shard_map/all_gather | solution.py:78
  246.8 6.9 %reduce_sum.19 = f32[64,64]{1,0:T(8,128)S(1)} reduce(f32[512,64,64]{2,1,0:T(8,128)} %all-gather.2.cloned.1.call-done, f32[]{:T(128)} %constant.62.clone.1), dimensions={0}, to_apply=%region_1.0 | reduce | flops 2093056 | bytes 8404996 | tf_op jit(solution)/shard_map/reduce_sum | solution.py:78
  254.7 4.4 %cholesky.16 = f32[48,48]{1,0:T(8,128)S(1)} custom-call(f32[48,48]{1,0:T(8,128)S(1)} %fusion.18), custom_call_target="Cholesky" | custom-call | tf_op jit(solution)/shard_map/jit(cholesky)/cholesky | solution.py:88
  260.6 3.7 %custom-call.10 = f32[1,48,48]{1,2,0:T(8,128)S(1)} custom-call(f32[1,48,48]{2,1,0:T(8,128)S(1)} %fusion.13), custom_call_target="InvertDiagBlocksLowerTriangular" | custom-call | tf_op jit(solution)/shard_map/jit(_cho_solve)/triangular_solve | solution.py:89
  271.8 3.4 %collective-permute-start.16 = (f32[1,16,512]{2,1,0:T(8,128)S(1)}, f32[1,16,512]{2,1,0:T(8,128)S(1)}, u32[]{:S(2)}, u32[]{:S(2)}) collective-permute-start(f32[1,16,512]{2,1,0:T(8,128)S(1)} %get-tuple-element.19), channel_id=1, source_target_pairs={{32,0},{64,32},{96,64},{128,96},{160,128},{192,160},{224,192},{256... | collective-permute-start | bytes 98312 | tf_op jit(solution)/shard_map/ppermute | solution.py:21
  277.9 3.8 %collective-permute-done.17 = f32[1,16,512]{2,1,0:T(8,128)S(1)} collective-permute-done((f32[1,16,512]{2,1,0:T(8,128)S(1)}, f32[1,16,512]{2,1,0:T(8,128)S(1)}, u32[]{:S(2)}, u32[]{:S(2)}) %collective-permute-start.17) | collective-permute-done | bytes 32800 | tf_op jit(solution)/shard_map/ppermute | solution.py:18
  281.7 4.9 %collective-permute-start.18 = (f32[10,1,512]{2,1,0:T(1,128)S(1)}, f32[10,1,512]{2,1,0:T(1,128)S(1)}, u32[]{:S(2)}, u32[]{:S(2)}) collective-permute-start(f32[10,1,512]{2,1,0:T(1,128)S(1)} %get-tuple-element.8), channel_id=1, source_target_pairs={{1,0},{2,1},{3,2},{4,3},{5,4},{6,5},{7,6},{8,7},{9,8},{10,9},{11,1... | collective-permute-start | bytes 61448 | tf_op jit(solution)/shard_map/ppermute | solution.py:21
  288.7 5.7 %collective-permute-done.19 = f32[10,1,512]{2,1,0:T(1,128)S(1)} collective-permute-done((f32[10,1,512]{2,1,0:T(1,128)S(1)}, f32[10,1,512]{2,1,0:T(1,128)S(1)}, u32[]{:S(2)}, u32[]{:S(2)}) %collective-permute-start.19) | collective-permute-done | bytes 20512 | tf_op jit(solution)/shard_map/ppermute | solution.py:18
  (114 shorter events, 56.1 us)
Async XLA Ops:
  7.2 239.7 %all-gather.2.cloned.1.call-start = ((), (), s32[]{:S(2)}) async-start(), calls=%async_computation | async-start | bytes 16809984 | tf_op jit(solution)/shard_map/all_gather | solution.py:78
  8.4 10.2 %collective-permute-start.1 = (f32[1,16,512]{2,1,0:T(8,128)S(1)}, f32[1,16,512]{2,1,0:T(8,128)S(1)}, u32[]{:S(2)}, u32[]{:S(2)}) collective-permute-start(f32[1,16,512]{2,1,0:T(8,128)S(1)} %slice.227), channel_id=1, source_target_pairs={{0,32},{32,64},{64,96},{96,128},{128,160},{160,192},{192,224},{224... | collective-permute-start | bytes 98312 | tf_op jit(solution)/shard_map/ppermute | solution.py:18
  10.4 9.4 %collective-permute-start = (f32[1,16,512]{2,1,0:T(8,128)S(1)}, f32[1,16,512]{2,1,0:T(8,128)S(1)}, u32[]{:S(2)}, u32[]{:S(2)}) collective-permute-start(f32[1,16,512]{2,1,0:T(8,128)S(1)} %slice.224), channel_id=1, source_target_pairs={{32,0},{64,32},{96,64},{128,96},{160,128},{192,160},{224,192},{256... | collective-permute-start | bytes 98312 | tf_op jit(solution)/shard_map/ppermute | solution.py:21
  19.8 20.2 %copy-start.5 = (f32[10,16,512]{2,1,0:T(8,128)}, f32[10,16,512]{2,1,0:T(8,128)S(1)}, u32[]{:S(2)}) copy-start(f32[10,16,512]{2,1,0:T(8,128)S(1)} %constant_dynamic-update-slice_fusion) | copy-start | bytes 983044
  20.5 23.8 %collective-permute-start.2 = (f32[10,1,512]{2,1,0:T(1,128)}, f32[10,1,512]{2,1,0:T(1,128)}, u32[]{:S(2)}, u32[]{:S(2)}) collective-permute-start(f32[10,1,512]{2,1,0:T(1,128)} %get-tuple-element.16), channel_id=1, source_target_pairs={{1,0},{2,1},{3,2},{4,3},{5,4},{6,5},{7,6},{8,7},{9,8},{10,9},{11,1... | collective-permute-start | bytes 61448 | tf_op jit(solution)/shard_map/ppermute | solution.py:21
  31.4 12.9 %collective-permute-start.3 = (f32[10,1,512]{2,1,0:T(1,128)}, f32[10,1,512]{2,1,0:T(1,128)}, u32[]{:S(2)}, u32[]{:S(2)}) collective-permute-start(f32[10,1,512]{2,1,0:T(1,128)} %get-tuple-element.17), channel_id=1, source_target_pairs={{0,1},{1,2},{2,3},{3,4},{4,5},{5,6},{6,7},{7,8},{8,9},{9,10},{10,1... | collective-permute-start | bytes 61448 | tf_op jit(solution)/shard_map/ppermute | solution.py:18
  46.4 4.3 %collective-permute-start.4 = (f32[1,16,512]{2,1,0:T(8,128)S(1)}, f32[1,16,512]{2,1,0:T(8,128)S(1)}, u32[]{:S(2)}, u32[]{:S(2)}) collective-permute-start(f32[1,16,512]{2,1,0:T(8,128)S(1)} %get-tuple-element.31), channel_id=1, source_target_pairs={{32,0},{64,32},{96,64},{128,96},{160,128},{192,160},{224,192},{256... | collective-permute-start | bytes 98312 | tf_op jit(solution)/shard_map/ppermute | solution.py:21
  48.3 6.4 %collective-permute-start.5 = (f32[1,16,512]{2,1,0:T(8,128)S(1)}, f32[1,16,512]{2,1,0:T(8,128)S(1)}, u32[]{:S(2)}, u32[]{:S(2)}) collective-permute-start(f32[1,16,512]{2,1,0:T(8,128)S(1)} %get-tuple-element.30), channel_id=1, source_target_pairs={{0,32},{32,64},{64,96},{96,128},{128,160},{160,192},{192,224},{224... | collective-permute-start | bytes 98312 | tf_op jit(solution)/shard_map/ppermute | solution.py:18
  54.8 8.3 %collective-permute-start.6 = (f32[10,1,512]{2,1,0:T(1,128)S(1)}, f32[10,1,512]{2,1,0:T(1,128)S(1)}, u32[]{:S(2)}, u32[]{:S(2)}) collective-permute-start(f32[10,1,512]{2,1,0:T(1,128)S(1)} %get-tuple-element.14), channel_id=1, source_target_pairs={{1,0},{2,1},{3,2},{4,3},{5,4},{6,5},{7,6},{8,7},{9,8},{10,9},{11,1... | collective-permute-start | bytes 61448 | tf_op jit(solution)/shard_map/ppermute | solution.py:21
  60.8 7.8 %collective-permute-start.7 = (f32[10,1,512]{2,1,0:T(1,128)S(1)}, f32[10,1,512]{2,1,0:T(1,128)S(1)}, u32[]{:S(2)}, u32[]{:S(2)}) collective-permute-start(f32[10,1,512]{2,1,0:T(1,128)S(1)} %get-tuple-element.15), channel_id=1, source_target_pairs={{0,1},{1,2},{2,3},{3,4},{4,5},{5,6},{6,7},{7,8},{8,9},{9,10},{10,1... | collective-permute-start | bytes 61448 | tf_op jit(solution)/shard_map/ppermute | solution.py:18
  68.9 4.3 %collective-permute-start.8 = (f32[1,16,512]{2,1,0:T(8,128)S(1)}, f32[1,16,512]{2,1,0:T(8,128)S(1)}, u32[]{:S(2)}, u32[]{:S(2)}) collective-permute-start(f32[1,16,512]{2,1,0:T(8,128)S(1)} %get-tuple-element.27), channel_id=1, source_target_pairs={{32,0},{64,32},{96,64},{128,96},{160,128},{192,160},{224,192},{256... | collective-permute-start | bytes 98312 | tf_op jit(solution)/shard_map/ppermute | solution.py:21
  70.9 6.4 %collective-permute-start.9 = (f32[1,16,512]{2,1,0:T(8,128)S(1)}, f32[1,16,512]{2,1,0:T(8,128)S(1)}, u32[]{:S(2)}, u32[]{:S(2)}) collective-permute-start(f32[1,16,512]{2,1,0:T(8,128)S(1)} %get-tuple-element.26), channel_id=1, source_target_pairs={{0,32},{32,64},{64,96},{96,128},{128,160},{160,192},{192,224},{224... | collective-permute-start | bytes 98312 | tf_op jit(solution)/shard_map/ppermute | solution.py:18
  77.4 6.0 %collective-permute-start.10 = (f32[10,1,512]{2,1,0:T(1,128)S(1)}, f32[10,1,512]{2,1,0:T(1,128)S(1)}, u32[]{:S(2)}, u32[]{:S(2)}) collective-permute-start(f32[10,1,512]{2,1,0:T(1,128)S(1)} %get-tuple-element.12), channel_id=1, source_target_pairs={{1,0},{2,1},{3,2},{4,3},{5,4},{6,5},{7,6},{8,7},{9,8},{10,9},{11,1... | collective-permute-start | bytes 61448 | tf_op jit(solution)/shard_map/ppermute | solution.py:21
  79.3 7.8 %collective-permute-start.11 = (f32[10,1,512]{2,1,0:T(1,128)S(1)}, f32[10,1,512]{2,1,0:T(1,128)S(1)}, u32[]{:S(2)}, u32[]{:S(2)}) collective-permute-start(f32[10,1,512]{2,1,0:T(1,128)S(1)} %get-tuple-element.13), channel_id=1, source_target_pairs={{0,1},{1,2},{2,3},{3,4},{4,5},{5,6},{6,7},{7,8},{8,9},{9,10},{10,1... | collective-permute-start | bytes 61448 | tf_op jit(solution)/shard_map/ppermute | solution.py:18
  87.4 4.4 %collective-permute-start.12 = (f32[1,16,512]{2,1,0:T(8,128)S(1)}, f32[1,16,512]{2,1,0:T(8,128)S(1)}, u32[]{:S(2)}, u32[]{:S(2)}) collective-permute-start(f32[1,16,512]{2,1,0:T(8,128)S(1)} %get-tuple-element.23), channel_id=1, source_target_pairs={{32,0},{64,32},{96,64},{128,96},{160,128},{192,160},{224,192},{256... | collective-permute-start | bytes 98312 | tf_op jit(solution)/shard_map/ppermute | solution.py:21
  89.3 6.4 %collective-permute-start.13 = (f32[1,16,512]{2,1,0:T(8,128)S(1)}, f32[1,16,512]{2,1,0:T(8,128)S(1)}, u32[]{:S(2)}, u32[]{:S(2)}) collective-permute-start(f32[1,16,512]{2,1,0:T(8,128)S(1)} %get-tuple-element.22), channel_id=1, source_target_pairs={{0,32},{32,64},{64,96},{96,128},{128,160},{160,192},{192,224},{224... | collective-permute-start | bytes 98312 | tf_op jit(solution)/shard_map/ppermute | solution.py:18
  91.8 20.9 %copy-start.3 = (f32[512,128]{1,0:T(8,128)}, f32[512,128]{1,0:T(8,128)S(1)}, u32[]{:S(2)}) copy-start(f32[512,128]{1,0:T(8,128)S(1)} %reshape.154) | copy-start | bytes 786436
  91.8 20.9 %copy-start.2 = (f32[512,128]{1,0:T(8,128)}, f32[512,128]{1,0:T(8,128)S(1)}, u32[]{:S(2)}) copy-start(f32[512,128]{1,0:T(8,128)S(1)} %reshape.155) | copy-start | bytes 786436
  95.8 6.0 %collective-permute-start.14 = (f32[10,1,512]{2,1,0:T(1,128)S(1)}, f32[10,1,512]{2,1,0:T(1,128)S(1)}, u32[]{:S(2)}, u32[]{:S(2)}) collective-permute-start(f32[10,1,512]{2,1,0:T(1,128)S(1)} %get-tuple-element.10), channel_id=1, source_target_pairs={{1,0},{2,1},{3,2},{4,3},{5,4},{6,5},{7,6},{8,7},{9,8},{10,9},{11,1... | collective-permute-start | bytes 61448 | tf_op jit(solution)/shard_map/ppermute | solution.py:21
  97.8 7.8 %collective-permute-start.15 = (f32[10,1,512]{2,1,0:T(1,128)S(1)}, f32[10,1,512]{2,1,0:T(1,128)S(1)}, u32[]{:S(2)}, u32[]{:S(2)}) collective-permute-start(f32[10,1,512]{2,1,0:T(1,128)S(1)} %get-tuple-element.11), channel_id=1, source_target_pairs={{0,1},{1,2},{2,3},{3,4},{4,5},{5,6},{6,7},{7,8},{8,9},{9,10},{10,1... | collective-permute-start | bytes 61448 | tf_op jit(solution)/shard_map/ppermute | solution.py:18
  271.8 6.0 %collective-permute-start.16 = (f32[1,16,512]{2,1,0:T(8,128)S(1)}, f32[1,16,512]{2,1,0:T(8,128)S(1)}, u32[]{:S(2)}, u32[]{:S(2)}) collective-permute-start(f32[1,16,512]{2,1,0:T(8,128)S(1)} %get-tuple-element.19), channel_id=1, source_target_pairs={{32,0},{64,32},{96,64},{128,96},{160,128},{192,160},{224,192},{256... | collective-permute-start | bytes 98312 | tf_op jit(solution)/shard_map/ppermute | solution.py:21
  275.2 6.4 %collective-permute-start.17 = (f32[1,16,512]{2,1,0:T(8,128)S(1)}, f32[1,16,512]{2,1,0:T(8,128)S(1)}, u32[]{:S(2)}, u32[]{:S(2)}) collective-permute-start(f32[1,16,512]{2,1,0:T(8,128)S(1)} %get-tuple-element.18), channel_id=1, source_target_pairs={{0,32},{32,64},{64,96},{96,128},{128,160},{160,192},{192,224},{224... | collective-permute-start | bytes 98312 | tf_op jit(solution)/shard_map/ppermute | solution.py:18
  281.7 7.0 %collective-permute-start.18 = (f32[10,1,512]{2,1,0:T(1,128)S(1)}, f32[10,1,512]{2,1,0:T(1,128)S(1)}, u32[]{:S(2)}, u32[]{:S(2)}) collective-permute-start(f32[10,1,512]{2,1,0:T(1,128)S(1)} %get-tuple-element.8), channel_id=1, source_target_pairs={{1,0},{2,1},{3,2},{4,3},{5,4},{6,5},{7,6},{8,7},{9,8},{10,9},{11,1... | collective-permute-start | bytes 61448 | tf_op jit(solution)/shard_map/ppermute | solution.py:21
  286.6 7.8 %collective-permute-start.19 = (f32[10,1,512]{2,1,0:T(1,128)S(1)}, f32[10,1,512]{2,1,0:T(1,128)S(1)}, u32[]{:S(2)}, u32[]{:S(2)}) collective-permute-start(f32[10,1,512]{2,1,0:T(1,128)S(1)} %get-tuple-element.9), channel_id=1, source_target_pairs={{0,1},{1,2},{2,3},{3,4},{4,5},{5,6},{6,7},{7,8},{8,9},{9,10},{10,1... | collective-permute-start | bytes 61448 | tf_op jit(solution)/shard_map/ppermute | solution.py:18
  (3 other events, 49.6 us)
Sparse Core Ops, SparseCore 0:
  118.3 128.4 all-gather.1
